TPU v7x, 128 devices: a whole 4x4x4 slice. The times are simulated.
128 devices in a mesh: ctx: 8 (over y, core), req: 16 (over x, z).
Axes of the slice: x: 4, y: 4, z: 4, core: 2. Of those that a mesh axis runs over, the one named last changes fastest.
Arguments:
- queries: bfloat16 [16, 512, 1024], P('req', 'ctx'), may hold values from -6 to 6
- keys: bfloat16 [16, 512, 1024], P('req', 'ctx'), may hold values from -6 to 6
- values: bfloat16 [16, 512, 2048], P('req', 'ctx'), may hold values from -6 to 6
- gate_input: bfloat16 [16, 512, 2048], P('req', 'ctx'), may hold values from -6 to 6
- beta: float32 [16, 16, 512], P('req', None, 'ctx'), may hold values from 0.05 to 1
- log_decay: float32 [16, 16, 512], P('req', None, 'ctx'), may hold values from -1 to 0
- norm_gain: float32 [128], replicated, may hold values from 0.1 to 1.9
- w_out: bfloat16 [2048, 2048], replicated, may hold values from -0.125 to 0.125
- hidden: bfloat16 [16, 512, 2048], P('req', 'ctx'), may hold values from -6 to 6
- post_gain: float32 [2048], replicated, may hold values from 0.1 to 1.9
- routes: int32 [16, 512, 10], P('req', 'ctx'), may hold values from 0 to 255, all different within a row; in each aligned block of 64 rows (0 to 63, 64 to 127, ..., all dimensions but the last counted through in order) at most 3 rows name the same one
- route_scores: float32 [16, 512, 10], P('req', 'ctx'), may hold values from 0.1 to 1
- expert_gate_up: bfloat16 [256, 2048, 1024], P(('ctx', 'req')), may hold values from -0.125 to 0.125
- expert_down: bfloat16 [256, 512, 2048], P(('ctx', 'req')), may hold values from -0.25 to 0.25
- accepted: int32 [16], P('req'), may hold values from 1 to 512
Outputs:
- layer_out: bfloat16 [16, 512, 2048], P('req', 'ctx')
- final_state: float32 [16, 16, 128, 128], P('req', 'ctx')
Inputs may be any that keep to these rules, and one draw needn't show every extreme that they name: A position's routes name different experts. Among the 64 positions of one device, no expert is named by more than 3 routes, a bound that some block reaches.
All inputs are finite; a program needn't handle non-finite values.
Results may differ from a plain program's by a relative error of at most 0.008.
Values may be sent and summed in bfloat16 or wider, within the bound.
No kernel may reach another device: no remote copies, remote signals or barrier semaphores. Data moves between devices by JAX's collectives and lax.ppermute only.
A program may use at most 128 MiB of HBM per device.

v0:
```python
import jax
import jax.numpy as jnp
from jax import lax
from jax.sharding import PartitionSpec as P

D = 2048
HK = 8
HV = 16
DK = 128
DV = 128
FFE = 512
TOPK = 10
EXP_DEV = 2


def unit_rows(x):
    x = x.astype(jnp.float32)
    return x * lax.rsqrt(jnp.sum(x * x, axis=-1, keepdims=True) + 1e-06)


def unit_lower_inverse(lower):
    highest = lax.Precision.HIGHEST
    n = lower.shape[-1]
    rows = jnp.arange(n)[:, None]
    cols = jnp.arange(n)[None, :]
    inv = None
    b = 1
    while b < n:
        sel = (rows // (2 * b) == cols // (2 * b)) & ((rows // b) % 2 == 1) & ((cols // b) % 2 == 0)
        c = jnp.where(sel, lower, 0.0)
        if inv is None:
            inv = lax.optimization_barrier(jnp.eye(n, dtype=lower.dtype) - c)
        else:
            mc = jnp.einsum("...ij,...jk->...ik", inv, c, precision=highest)
            inv = inv - jnp.einsum("...ij,...jk->...ik", mc, inv, precision=highest)
        b *= 2
    return inv


def run_experts(arrived, expert_gate_up, expert_down):
    provider_rows, count, part, width = arrived.shape
    rows = arrived.transpose(1, 0, 2, 3).reshape(count, provider_rows * part, width)
    both = jnp.einsum("erd,edf->erf", rows, expert_gate_up, preferred_element_type=jnp.float32)
    inner = (jax.nn.silu(both[..., :FFE]) * both[..., FFE:]).astype(jnp.bfloat16)
    result = jnp.einsum(
        "erf,efd->erd", inner, expert_down, preferred_element_type=jnp.float32
    ).astype(jnp.bfloat16)
    return result.reshape(count, provider_rows, part, width).transpose(1, 0, 2, 3)


def shards(
    queries,
    keys,
    values,
    gate_input,
    beta,
    log_decay,
    norm_gain,
    w_out,
    hidden,
    post_gain,
    routes,
    route_scores,
    expert_gate_up,
    expert_down,
    accepted,
):
    highest = lax.Precision.HIGHEST
    seq = queries.shape[1]
    n_ctx = lax.axis_size("ctx")
    n_req = lax.axis_size("req")
    n_dev = n_ctx * n_req
    experts = EXP_DEV * n_dev
    cap = max(2, 3 * seq * TOPK // (2 * experts))
    kh_dev = HK // n_ctx
    hv_dev = HV // n_ctx
    qw = kh_dev * DK
    vw = hv_dev * DV

    packed = jnp.concatenate(
        [
            queries[0].reshape(seq, n_ctx, qw),
            keys[0].reshape(seq, n_ctx, qw),
            values[0].reshape(seq, n_ctx, vw),
            gate_input[0].reshape(seq, n_ctx, vw),
        ],
        axis=2,
    ).transpose(1, 0, 2)
    arrived = lax.all_to_all(packed, "ctx", 0, 0, tiled=True)
    rates_decay = (
        jnp.stack([beta[0], log_decay[0]]).reshape(2, n_ctx, hv_dev, seq).transpose(1, 0, 2, 3)
    )
    rd = lax.all_to_all(rates_decay, "ctx", 0, 0, tiled=True)
    rates = rd[:, 0].transpose(1, 0, 2)
    gamma = jnp.cumsum(rd[:, 1].transpose(1, 0, 2), axis=-1)
    qc = unit_rows(arrived[..., :qw]) * DK ** (-0.5)
    kc = unit_rows(arrived[..., qw : 2 * qw])
    vc = (
        arrived[..., 2 * qw : 2 * qw + vw]
        .astype(jnp.float32)
        .reshape(n_ctx, seq, hv_dev, DV)
        .transpose(2, 0, 1, 3)
    )
    gc = arrived[..., 2 * qw + vw :].reshape(n_ctx, seq, hv_dev, DV)

    ordinals = jnp.arange(seq)
    before = ordinals[:, None] > ordinals[None, :]
    upto = ordinals[:, None] >= ordinals[None, :]
    spans = gamma[..., :, None] - gamma[..., None, :]
    pair_decay = jnp.exp(jnp.where(upto, spans, 0.0))
    key_key = jnp.einsum("ntd,nsd->nts", kc, kc, precision=highest)
    lower = jnp.where(before, pair_decay * key_key[None] * rates[..., None, :], 0.0)
    inverse = unit_lower_inverse(lower)
    growth = jnp.exp(gamma)
    right = jnp.concatenate(
        [vc, growth[..., None] * jnp.broadcast_to(kc[None], vc.shape)], axis=-1
    )
    solved = jnp.einsum("hnts,hnsf->hntf", inverse, right, precision=highest)
    solved_values = solved[..., :DV]
    solved_keys = solved[..., DV:]
    tail = rates * jnp.exp(gamma[..., -1:] - gamma)
    weighted = kc[None] * tail[..., None]
    identity = jnp.eye(DK, dtype=jnp.float32)
    transfer = growth[..., -1, None, None] * identity - jnp.einsum(
        "hntd,hnte->hnde", weighted, solved_keys, precision=highest
    )
    offset = jnp.einsum("hntd,hnte->hnde", weighted, solved_values, precision=highest)
    state = jnp.zeros((hv_dev, DK, DV), jnp.float32)
    states = [state]
    for n in range(n_ctx - 1):
        state = offset[:, n] + jnp.einsum(
            "hde,hef->hdf", transfer[:, n], state, precision=highest
        )
        states.append(state)
    states = jnp.stack(states, axis=1)
    pseudo = solved_values - jnp.einsum("hntd,hnde->hnte", solved_keys, states, precision=highest)
    query_key = jnp.einsum("ntd,nsd->nts", qc, kc, precision=highest)
    mixing = jnp.where(upto, pair_decay * query_key[None] * rates[..., None, :], 0.0)
    core = growth[..., None] * jnp.einsum("ntd,hnde->hnte", qc, states, precision=highest)
    core = core + jnp.einsum("hnts,hnse->hnte", mixing, pseudo, precision=highest)

    last = accepted[0] - 1
    chunk = last // seq
    local = last % seq
    gamma_chunk = lax.dynamic_index_in_dim(gamma, chunk, axis=1, keepdims=False)
    rates_chunk = lax.dynamic_index_in_dim(rates, chunk, axis=1, keepdims=False)
    pseudo_chunk = lax.dynamic_index_in_dim(pseudo, chunk, axis=1, keepdims=False)
    state_chunk = lax.dynamic_index_in_dim(states, chunk, axis=1, keepdims=False)
    keys_chunk = lax.dynamic_index_in_dim(kc, chunk, axis=0, keepdims=False)
    gamma_at = lax.dynamic_index_in_dim(gamma_chunk, local, axis=1, keepdims=False)
    keep = jnp.where(
        ordinals[None, :] <= local,
        rates_chunk * jnp.exp(jnp.minimum(gamma_at[:, None] - gamma_chunk, 0.0)),
        0.0,
    )
    final_state = jnp.exp(gamma_at)[:, None, None] * state_chunk + jnp.einsum(
        "td,hte->hde", keys_chunk, keep[..., None] * pseudo_chunk, precision=highest
    )
    final_state = final_state[None]

    scale = lax.rsqrt(jnp.mean(core * core, axis=-1, keepdims=True) + 1e-06)
    gating = jax.nn.silu(gc.astype(jnp.float32).transpose(2, 0, 1, 3))
    normed = (core * scale * norm_gain * gating).astype(jnp.bfloat16)
    normed = normed.transpose(1, 2, 0, 3).reshape(n_ctx, seq, vw)
    back = lax.all_to_all(normed, "ctx", 0, 0, tiled=True)
    resid = hidden[0].astype(jnp.float32) + jnp.einsum(
        "jtf,jfd->td",
        back,
        w_out.reshape(n_ctx, vw, D),
        preferred_element_type=jnp.float32,
    )
    moe_in = (
        resid * lax.rsqrt(jnp.mean(resid * resid, axis=-1, keepdims=True) + 1e-06) * post_gain
    ).astype(jnp.bfloat16)

    flat_ids = routes[0].reshape(-1)
    onehot = (flat_ids[:, None] == jnp.arange(experts, dtype=jnp.int32)[None, :]).astype(jnp.int32)
    earlier = jnp.cumsum(onehot, axis=0) - onehot
    slot = jnp.sum(earlier * onehot, axis=1)
    target = (flat_ids * cap + slot).reshape(seq, TOPK)
    slots = jnp.arange(experts * cap, dtype=jnp.int32)
    hits = target[None, :, :] == slots[:, None, None]
    dispatch = jnp.sum(jnp.where(hits, 1.0, 0.0), axis=-1).astype(jnp.bfloat16)
    outgoing_rows = jnp.dot(dispatch, moe_in, preferred_element_type=jnp.float32).astype(
        jnp.bfloat16
    )
    returned = lax.all_to_all(
        run_experts(
            lax.all_to_all(
                outgoing_rows.reshape(n_dev, EXP_DEV, cap, D),
                ("ctx", "req"),
                split_axis=0,
                concat_axis=0,
                tiled=True,
            ),
            expert_gate_up,
            expert_down,
        ),
        ("ctx", "req"),
        split_axis=0,
        concat_axis=0,
        tiled=True,
    )
    scores = route_scores[0]
    mix_weights = scores / jnp.sum(scores, axis=-1, keepdims=True)
    combine = jnp.sum(jnp.where(hits, mix_weights[None], 0.0), axis=-1).T
    moe_out = jnp.dot(
        combine,
        returned.reshape(experts * cap, D).astype(jnp.float32),
        precision=highest,
    )
    layer_out = (resid + moe_out).astype(jnp.bfloat16)[None]
    return (layer_out, final_state)


def solution(mesh):
    placed = (
        P("req", "ctx", None),
        P("req", "ctx", None),
        P("req", "ctx", None),
        P("req", "ctx", None),
        P("req", None, "ctx"),
        P("req", None, "ctx"),
        P(),
        P(),
        P("req", "ctx", None),
        P(),
        P("req", "ctx", None),
        P("req", "ctx", None),
        P(("ctx", "req"), None, None),
        P(("ctx", "req"), None, None),
        P("req"),
    )
    return jax.shard_map(
        shards,
        mesh=mesh,
        in_specs=placed,
        out_specs=(P("req", "ctx", None), P("req", "ctx", None, None)),
        check_vma=False,
    )
```

profile of v0, /device:TPU:1, one launch (start us, length us, event | category | flops | bytes accessed | tf_op | source)
XLA Modules:
  0.0 211.5 jit_solution(4934934420896496836)
XLA Ops:
  0.6 0.7 pad_maximum_fusion
  1.4 0.7 reshape.849
  2.0 6.0 %all-to-all-start = ((f32[8,1,256]{2,1,0:T(1,128)}), f32[8,1,256]{2,1,0:T(1,128)S(1)}, u32[]{:S(2)}, u32[]{:S(2)}) async-start(f32[8,1,256]{2,1,0:T(1,128)} %reshape.849), calls=%async_computation | async-start | bytes 16384 | tf_op jit(solution)/shard_map/all_to_all | solution.py:93
  8.1 0.7 broadcast_multiply_fusion.1
  8.8 0.8 copy.125
  10.1 0.9 copy.149
  11.1 0.9 copy.150
  12.0 1.0 copy.151
  13.1 1.0 copy.152
  14.7 0.3 fusion.23
  15.7 0.9 maximum_bitcast_fusion
  16.6 4.8 %all-to-all-start.1 = ((bf16[8,64,768]{2,1,0:T(8,128)(2,1)}), bf16[8,64,768]{2,1,0:T(8,128)(2,1)S(1)}, u32[]{:S(2)}, u32[]{:S(2)}) async-start(bf16[8,64,768]{2,1,0:T(8,128)(2,1)} %maximum_bitcast_fusion), calls=%async_computation.1 | async-start | bytes 1572864 | tf_op jit(solution)/shard_map/all_to_all | solution.py:89
  21.5 0.5 broadcast.1178
  22.0 0.7 reduce.9
  22.8 0.6 reduce_window_sum.26
  23.8 9.8 %all-to-all-done.1 = bf16[8,64,768]{2,1,0:T(8,128)(2,1)S(1)} async-done(((bf16[8,64,768]{2,1,0:T(8,128)(2,1)}), bf16[8,64,768]{2,1,0:T(8,128)(2,1)S(1)}, u32[]{:S(2)}, u32[]{:S(2)}) %all-to-all-start.1) | async-done | bytes 786464 | tf_op jit(solution)/shard_map/all_to_all | solution.py:89
  33.8 0.7 fusion.125
  34.5 0.2 select_subtract_fusion
  34.7 0.8 fusion.47
  35.6 0.6 convolution_subtract_fusion.5
  36.2 0.8 fusion.45
  37.1 0.6 convolution_subtract_fusion.4
  37.7 0.8 fusion.43
  38.6 0.6 convolution_subtract_fusion.3
  39.2 0.8 fusion.41
  40.1 0.6 convolution_subtract_fusion.2
  40.7 0.8 fusion.39
  41.6 0.6 convolution_subtract_fusion.1
  42.7 1.0 fusion.10
  43.7 2.0 fusion.20
  45.7 2.2 %convolution_subtract_fusion = f32[2,8,128,128]{3,2,1,0:T(8,128)S(1)} fusion(f32[128,128]{1,0:T(8,128)S(1)} %fusion.124, f32[2,8]{1,0:T(2,128)S(1)} %slice_reduce_fusion, f32[2,8,64,256]{3,2,1,0:T(8,128)S(1)} %fusion.10, f32[2,8,64]{2,1,0:T(8,128)S(1)} %get-tuple-element.23, f32[8,64,128]{2,1,0:T(8,128)S(1)} %convert_multiply_fusion.2), kind=kOutput, calls=%fused_computation.14 | convolution fusion | flops 201981952 | bytes 1909760 | tf_op jit(solution)/shard_map/hntd,hnte->hnde/dot_general | solution.py:124
  48.0 0.3 bitcast_dynamic-update-slice_fusion.5
  48.2 0.3 bitcast_dynamic-update-slice_fusion.4
  48.5 0.3 bitcast_dynamic-update-slice_fusion.3
  48.8 0.3 bitcast_dynamic-update-slice_fusion.2
  49.1 0.3 bitcast_dynamic-update-slice_fusion.1
  49.3 0.3 bitcast_dynamic-update-slice_fusion
  49.6 0.3 fusion.7
  49.9 1.1 convolution_subtract_fusion.6
  51.0 0.7 fusion.55
  51.7 0.8 fusion.58
  52.4 1.0 fusion.31
  53.5 1.1 copy_bitcast_fusion
  54.5 4.7 %all-to-all-start.2 = ((bf16[8,64,256]{2,1,0:T(8,128)(2,1)}), bf16[8,64,256]{2,1,0:T(8,128)(2,1)S(1)}, u32[]{:S(2)}, u32[]{:S(2)}) async-start(bf16[8,64,256]{2,1,0:T(8,128)(2,1)} %copy_bitcast_fusion), calls=%async_computation.2 | async-start | bytes 524288 | tf_op jit(solution)/shard_map/all_to_all | solution.py:165
  59.4 1.1 select_reduce_fusion
  60.4 5.3 %all-to-all-done.2 = bf16[8,64,256]{2,1,0:T(8,128)(2,1)S(1)} async-done(((bf16[8,64,256]{2,1,0:T(8,128)(2,1)}), bf16[8,64,256]{2,1,0:T(8,128)(2,1)S(1)}, u32[]{:S(2)}, u32[]{:S(2)}) %all-to-all-start.2) | async-done | bytes 262176 | tf_op jit(solution)/shard_map/all_to_all | solution.py:165
  65.7 5.1 %multiply_reduce_fusion = (f32[64]{0:T(128)S(1)}, f32[64,2048]{1,0:T(8,128)S(1)}) fusion(bf16[8,64,256]{2,1,0:T(8,128)(2,1)S(1)} %all-to-all-done.2, bf16[8,256,2048]{2,1,0:T(8,128)(2,1)} %bitcast.266, bf16[1,64,2048]{2,1,0:T(8,128)(2,1)S(1)} %copy-done.4), kind=kOutput, calls=%fused_computation.69 | convolution fusion | flops 537395136 | bytes 9437440 | tf_op jit(solution)/shard_map/jtf,jfd->td/dot_general | solution.py:166
  70.8 0.8 copy-done.1
  71.6 1.0 convolution_convert_fusion
  72.7 4.4 %reshape.835 = bf16[128,2,3,2048]{3,2,1,0:T(4,128)(2,1)} reshape(bf16[768,2048]{1,0:T(8,128)(2,1)S(1)} %convolution_convert_fusion) | data formatting | bytes 6291456 | tf_op jit(solution)/shard_map/reshape | solution.py:190
  77.1 8.5 %copy.131 = bf16[128,2,3,2048]{3,1,2,0:T(2,128)(2,1)S(1)} copy(bf16[128,2,3,2048]{3,2,1,0:T(4,128)(2,1)} %reshape.835) | data formatting | bytes 6291456 | tf_op jit(solution)/shard_map/reshape | solution.py:190
  85.6 49.9 %all_to_all.25 = bf16[128,2,3,2048]{3,1,2,0:T(2,128)(2,1)S(1)} all-to-all(bf16[128,2,3,2048]{3,1,2,0:T(2,128)(2,1)S(1)} %copy.131), channel_id=1, replica_groups=mesh['ctx'=8,'req'=16] {'ctx','req'}, dimensions={0} | all-to-all | bytes 6291456 | tf_op jit(solution)/shard_map/all_to_all | solution.py:189
  135.5 6.9 %fusion = f32[2,384,1024]{2,1,0:T(8,128)S(1)} fusion(bf16[2,2048,1024]{2,1,0:T(8,128)(2,1)} %param.27, bf16[2,384,2048]{2,0,1:T(2,128)(2,1)S(1)} %bitcast.268), kind=kOutput, calls=%fused_computation.2 | convolution fusion | flops 3221225472 | bytes 14680064 | tf_op jit(solution)/shard_map/erd,edf->erf/dot_general | solution.py:43
  142.4 1.9 convolution_convert_fusion.1
  144.3 4.9 %copy.133 = bf16[2,384,2048]{2,0,1:T(2,128)(2,1)} copy(bf16[2,384,2048]{2,1,0:T(8,128)(2,1)S(1)} %convolution_convert_fusion.1) | data formatting | bytes 6291456 | tf_op jit(solution)/shard_map/convert_element_type | solution.py:47
  149.2 5.0 %all-to-all-start.4 = ((bf16[128,2,3,2048]{3,1,2,0:T(2,128)(2,1)}), bf16[128,2,3,2048]{3,1,2,0:T(2,128)(2,1)S(1)}, u32[]{:S(2)}, u32[]{:S(2)}) async-start(bf16[128,2,3,2048]{3,1,2,0:T(2,128)(2,1)} %bitcast.267), calls=%async_computation.4 | async-start | bytes 6291456 | tf_op jit(solution)/shard_map/all_to_all | solution.py:187
  155.2 1.6 dynamic-slice_bitcast_fusion
  156.7 1.0 copy.135
  157.7 2.0 fusion.9
  159.7 1.7 copy.136
  161.4 33.6 %all-to-all-done.4 = bf16[128,2,3,2048]{3,1,2,0:T(2,128)(2,1)S(1)} async-done(((bf16[128,2,3,2048]{3,1,2,0:T(2,128)(2,1)}), bf16[128,2,3,2048]{3,1,2,0:T(2,128)(2,1)S(1)}, u32[]{:S(2)}, u32[]{:S(2)}) %all-to-all-start.4) | async-done | bytes 3145760 | tf_op jit(solution)/shard_map/all_to_all | solution.py:187
  195.0 5.2 %copy.134 = bf16[128,2,3,2048]{3,2,1,0:T(4,128)(2,1)} copy(bf16[128,2,3,2048]{3,1,2,0:T(2,128)(2,1)S(1)} %all-to-all-done.4) | data formatting | bytes 6291456 | tf_op jit(solution)/shard_map/all_to_all | solution.py:187
  200.2 7.5 %reshape.838 = bf16[768,2048]{1,0:T(8,128)(2,1)S(1)} reshape(bf16[128,2,3,2048]{3,2,1,0:T(4,128)(2,1)} %copy.134) | data formatting | bytes 6291456 | tf_op jit(solution)/shard_map/reshape | solution.py:209
  207.8 3.5 %fusion.4 = bf16[1,64,2048]{2,1,0:T(8,128)(2,1)} fusion(f32[64,2048]{1,0:T(8,128)} %copy-done.1, f32[768,64]{0,1:T(8,128)S(1)} %copy-done.3, bf16[768,2048]{1,0:T(8,128)(2,1)S(1)} %reshape.838), kind=kOutput, calls=%fused_computation.8 | convolution fusion | flops 1208221696 | bytes 4128768 | tf_op jit(solution)/shard_map/dot_general | solution.py:207
  (79 shorter events, 3.5 us)
Async XLA Ops:
  2.0 14.6 %all-to-all-start = ((f32[8,1,256]{2,1,0:T(1,128)}), f32[8,1,256]{2,1,0:T(1,128)S(1)}, u32[]{:S(2)}, u32[]{:S(2)}) async-start(f32[8,1,256]{2,1,0:T(1,128)} %reshape.849), calls=%async_computation | async-start | bytes 16384 | tf_op jit(solution)/shard_map/all_to_all | solution.py:93
  14.5 7.0 %copy-start.5 = (f32[1,64,10]{1,0,2:T(1,128)S(1)}, f32[1,64,10]{1,0,2:T(1,128)}, u32[]{:S(2)}) copy-start(f32[1,64,10]{1,0,2:T(1,128)} %param.26) | copy-start | bytes 7684
  16.6 17.0 %all-to-all-start.1 = ((bf16[8,64,768]{2,1,0:T(8,128)(2,1)}), bf16[8,64,768]{2,1,0:T(8,128)(2,1)S(1)}, u32[]{:S(2)}, u32[]{:S(2)}) async-start(bf16[8,64,768]{2,1,0:T(8,128)(2,1)} %maximum_bitcast_fusion), calls=%async_computation.1 | async-start | bytes 1572864 | tf_op jit(solution)/shard_map/all_to_all | solution.py:89
  49.9 4.7 %copy-start = (f32[2,8,128,128]{3,2,0,1:T(8,128)}, f32[2,8,128,128]{3,2,0,1:T(8,128)S(1)}, u32[]{:S(2)}) copy-start(f32[2,8,128,128]{3,2,0,1:T(8,128)S(1)} %fusion.7) | copy-start | bytes 3145732
  49.9 3.6 %copy-start.7 = (f32[128]{0:T(128)S(1)}, f32[128]{0:T(128)}, u32[]{:S(2)}) copy-start(f32[128]{0:T(128)} %param.21) | copy-start | bytes 1540
  51.0 3.6 %copy-start.2 = (f32[2,8,64,128]{3,2,1,0:T(8,128)}, f32[2,8,64,128]{3,2,1,0:T(8,128)S(1)}, u32[]{:S(2)}) copy-start(f32[2,8,64,128]{3,2,1,0:T(8,128)S(1)} %convolution_subtract_fusion.6) | copy-start | bytes 1572868
  52.4 13.3 %copy-start.4 = (bf16[1,64,2048]{2,1,0:T(8,128)(2,1)S(1)}, bf16[1,64,2048]{2,1,0:T(8,128)(2,1)}, u32[]{:S(2)}) copy-start(bf16[1,64,2048]{2,1,0:T(8,128)(2,1)} %param.23) | copy-start | bytes 786436
  54.5 11.2 %all-to-all-start.2 = ((bf16[8,64,256]{2,1,0:T(8,128)(2,1)}), bf16[8,64,256]{2,1,0:T(8,128)(2,1)S(1)}, u32[]{:S(2)}, u32[]{:S(2)}) async-start(bf16[8,64,256]{2,1,0:T(8,128)(2,1)} %copy_bitcast_fusion), calls=%async_computation.2 | async-start | bytes 524288 | tf_op jit(solution)/shard_map/all_to_all | solution.py:165
  65.7 5.9 %copy-start.6 = (f32[2048]{0:T(1024)S(1)}, f32[2048]{0:T(1024)}, u32[]{:S(2)}) copy-start(f32[2048]{0:T(1024)} %param.24) | copy-start | bytes 24580
  70.8 0.8 copy-start.1
  135.5 6.9 %copy-start.8 = (bf16[2,512,2048]{2,1,0:T(8,128)(2,1)S(1)}, bf16[2,512,2048]{2,1,0:T(8,128)(2,1)}, u32[]{:S(2)}) copy-start(bf16[2,512,2048]{2,1,0:T(8,128)(2,1)} %param.28) | copy-start | bytes 12582916
  149.2 45.8 %all-to-all-start.4 = ((bf16[128,2,3,2048]{3,1,2,0:T(2,128)(2,1)}), bf16[128,2,3,2048]{3,1,2,0:T(2,128)(2,1)S(1)}, u32[]{:S(2)}, u32[]{:S(2)}) async-start(bf16[128,2,3,2048]{3,1,2,0:T(2,128)(2,1)} %bitcast.267), calls=%async_computation.4 | async-start | bytes 6291456 | tf_op jit(solution)/shard_map/all_to_all | solution.py:187
  200.2 7.6 %copy-start.3 = (f32[768,64]{0,1:T(8,128)S(1)}, f32[768,64]{0,1:T(8,128)}, u32[]{:S(2)}) copy-start(f32[768,64]{0,1:T(8,128)} %get-tuple-element.15) | copy-start | bytes 589828
where the time goes:
time: 215 us; the launch traced here: 212 us
  blocking collectives  49.9 us (23%)
  waiting for transfers between devices  48.7 us (23%)
  local copies, waits for them, and re-layouts  43.2 us (20%)
  matrix products  39 us (18%)
  starting transfers between devices  20.5 us (10%)
  other arithmetic  8 us (4%)
  between operations  2.25 us (1%)
    all_to_all x1, blocking collectives, shards(): lax.all_to_all(outgoing_rows.reshape(n_dev, EXP_DEV, cap, D), ('ctx', 're...  49.9 us
    all_to_all x1, waiting for transfers between devices, shards(): lax.all_to_all(run_experts(lax.all_to_all(outgoing_rows.reshape(n_dev, EX...  33.6 us
    reshape x2, local copies, waits for them, and re-layouts, shards(): outgoing_rows.reshape(n_dev, EXP_DEV, cap, D)  12.9 us
    all_to_all x1, waiting for transfers between devices, shards(): arrived = lax.all_to_all(packed, 'ctx', 0, 0, tiled=True)  9.79 us
    unnamed x29, local copies, waits for them, and re-layouts  7.91 us
    reshape x1, local copies, waits for them, and re-layouts, shards(): returned.reshape(experts * cap, D).astype(jnp.float32)  7.55 us
    dot_general x1, matrix products, run_experts(): jnp.einsum('erd,edf->erf', rows, expert_gate_up, preferred_element_type=j...  6.86 us
    all_to_all x1, starting transfers between devices, shards(): rd = lax.all_to_all(rates_decay, 'ctx', 0, 0, tiled=True)  5.96 us
  transfers between devices with their start and end apart: 4, of which 3 were waited for; matrix products, arithmetic and copies ran while one was open for 9% of the time, Pallas kernels for 0%

commit v1 on v0

--- a/solution.py
+++ b/solution.py
@@ -178,35 +178,34 @@
     earlier = jnp.cumsum(onehot, axis=0) - onehot
     slot = jnp.sum(earlier * onehot, axis=1)
     target = (flat_ids * cap + slot).reshape(seq, TOPK)
-    slots = jnp.arange(experts * cap, dtype=jnp.int32)
-    hits = target[None, :, :] == slots[:, None, None]
+    slots = (
+        jnp.arange(experts * cap, dtype=jnp.int32)
+        .reshape(n_dev, EXP_DEV, cap)
+        .transpose(0, 2, 1)
+    )
+    hits = target[None, None, None, :, :] == slots[..., None, None]
     dispatch = jnp.sum(jnp.where(hits, 1.0, 0.0), axis=-1).astype(jnp.bfloat16)
-    outgoing_rows = jnp.dot(dispatch, moe_in, preferred_element_type=jnp.float32).astype(
-        jnp.bfloat16
-    )
-    returned = lax.all_to_all(
-        run_experts(
-            lax.all_to_all(
-                outgoing_rows.reshape(n_dev, EXP_DEV, cap, D),
-                ("ctx", "req"),
-                split_axis=0,
-                concat_axis=0,
-                tiled=True,
-            ),
-            expert_gate_up,
-            expert_down,
-        ),
-        ("ctx", "req"),
-        split_axis=0,
-        concat_axis=0,
-        tiled=True,
-    )
+    outgoing_rows = jnp.einsum(
+        "dcet,tf->dcef", dispatch, moe_in, preferred_element_type=jnp.float32
+    ).astype(jnp.bfloat16)
+    arrived_rows = lax.all_to_all(
+        outgoing_rows, ("ctx", "req"), split_axis=0, concat_axis=0, tiled=True
+    )
+    both = jnp.einsum(
+        "scex,exf->escf", arrived_rows, expert_gate_up, preferred_element_type=jnp.float32
+    )
+    inner = (jax.nn.silu(both[..., :FFE]) * both[..., FFE:]).astype(jnp.bfloat16)
+    result = jnp.einsum(
+        "escf,efx->scex", inner, expert_down, preferred_element_type=jnp.float32
+    ).astype(jnp.bfloat16)
+    returned = lax.all_to_all(result, ("ctx", "req"), split_axis=0, concat_axis=0, tiled=True)
     scores = route_scores[0]
     mix_weights = scores / jnp.sum(scores, axis=-1, keepdims=True)
-    combine = jnp.sum(jnp.where(hits, mix_weights[None], 0.0), axis=-1).T
-    moe_out = jnp.dot(
+    combine = jnp.sum(jnp.where(hits, mix_weights, 0.0), axis=-1)
+    moe_out = jnp.einsum(
+        "dcet,dcex->tx",
         combine,
-        returned.reshape(experts * cap, D).astype(jnp.float32),
+        returned.astype(jnp.float32),
         precision=highest,
     )
     layer_out = (resid + moe_out).astype(jnp.bfloat16)[None]

time: 215 us -> 189 us (0.88)
  local copies, waits for them, and re-layouts: 43.2 us -> 19.7 us
    reshape x3 -> x0, local copies, waits for them, and re-layouts: 20.4 us -> none  [the longest x2 12.9 us: shards(): outgoing_rows.reshape(n_dev, EXP_DEV, cap, D)]
    all_to_all x1 -> x0, local copies, waits for them, and re-layouts: 5.22 us -> none  [shards(): lax.all_to_all(run_experts(lax.all_to_all(outgoing_rows.reshape(n_dev, EX...]
    convert_element_type x1 -> x2, local copies, waits for them, and re-layouts: 4.9 us -> 8.14 us  [the longest x1 4.9 us: shards(): result = jnp.einsum('escf,efx->scex', inner, expert_down, preferred_eleme...]
    unnamed x29 -> x32, local copies, waits for them, and re-layouts: 7.91 us -> 7 us
where the time goes in v1:
time: 189 us; the launch traced here: 186 us
  blocking collectives  50.1 us (27%)
  waiting for transfers between devices  48.8 us (26%)
  matrix products  37.8 us (20%)
  starting transfers between devices  20 us (11%)
  local copies, waits for them, and re-layouts  19.7 us (10%)
  other arithmetic  7.32 us (4%)
  between operations  2.2 us (1%)
    all_to_all x1, blocking collectives, shards(): lax.all_to_all(outgoing_rows, ('ctx', 'req'), split_axis=0, concat_axis=0...  50.1 us
    all_to_all x1, waiting for transfers between devices, shards(): lax.all_to_all(result, ('ctx', 'req'), split_axis=0, concat_axis=0, tiled...  33.6 us
    all_to_all x1, waiting for transfers between devices, shards(): arrived = lax.all_to_all(packed, 'ctx', 0, 0, tiled=True)  9.83 us
    unnamed x32, local copies, waits for them, and re-layouts  7 us
    all_to_all x1, starting transfers between devices, shards(): rd = lax.all_to_all(rates_decay, 'ctx', 0, 0, tiled=True)  5.96 us
    all_to_all x1, waiting for transfers between devices, shards(): back = lax.all_to_all(normed, 'ctx', 0, 0, tiled=True)  5.36 us
    dot_general x1, matrix products, shards(): jnp.einsum('jtf,jfd->td', back, w_out.reshape(n_ctx, vw, D), preferred_el...  5.08 us
    dot_general x1, matrix products, shards(): jnp.einsum('dcet,dcex->tx', combine, returned.astype(jnp.float32), precis...  5.08 us
  transfers between devices with their start and end apart: 4, of which 3 were waited for; matrix products, arithmetic and copies ran while one was open for 9% of the time, Pallas kernels for 0%

profile of v1, /device:TPU:1, one launch (start us, length us, event | category | flops | bytes accessed | tf_op | source)
XLA Modules:
  0.0 186.0 jit_solution(10768445943531338116)
XLA Ops:
  0.6 0.8 pad_maximum_fusion
  1.4 0.7 reshape.881
  2.1 6.0 %all-to-all-start = ((f32[8,1,256]{2,1,0:T(1,128)}), f32[8,1,256]{2,1,0:T(1,128)S(1)}, u32[]{:S(2)}, u32[]{:S(2)}) async-start(f32[8,1,256]{2,1,0:T(1,128)} %reshape.881), calls=%async_computation | async-start | bytes 16384 | tf_op jit(solution)/shard_map/all_to_all | solution.py:93
  8.2 0.8 copy.153
  9.2 1.0 copy.183
  10.3 1.0 copy.184
  11.4 0.9 copy.181
  12.5 0.2 fusion.38
  12.8 0.2 copy.157
  13.1 0.3 fusion.45
  14.1 0.9 maximum_bitcast_fusion
  15.0 4.8 %all-to-all-start.1 = ((bf16[8,64,768]{2,1,0:T(8,128)(2,1)}), bf16[8,64,768]{2,1,0:T(8,128)(2,1)S(1)}, u32[]{:S(2)}, u32[]{:S(2)}) async-start(bf16[8,64,768]{2,1,0:T(8,128)(2,1)} %maximum_bitcast_fusion), calls=%async_computation.1 | async-start | bytes 1572864 | tf_op jit(solution)/shard_map/all_to_all | solution.py:89
  19.9 0.5 broadcast.1193
  20.4 0.7 reduce.9
  21.2 0.6 reduce_window_sum.26
  22.2 9.8 %all-to-all-done.1 = bf16[8,64,768]{2,1,0:T(8,128)(2,1)S(1)} async-done(((bf16[8,64,768]{2,1,0:T(8,128)(2,1)}), bf16[8,64,768]{2,1,0:T(8,128)(2,1)S(1)}, u32[]{:S(2)}, u32[]{:S(2)}) %all-to-all-start.1) | async-done | bytes 786464 | tf_op jit(solution)/shard_map/all_to_all | solution.py:89
  32.0 0.2 fusion.75
  32.2 0.7 fusion.149
  32.9 0.2 select_subtract_fusion
  33.2 0.8 fusion.69
  34.0 0.6 convolution_subtract_fusion.5
  34.7 0.8 fusion.67
  35.5 0.6 convolution_subtract_fusion.4
  36.1 0.8 fusion.65
  37.0 0.6 convolution_subtract_fusion.3
  37.6 0.8 fusion.63
  38.5 0.6 convolution_subtract_fusion.2
  39.1 0.8 fusion.61
  40.0 0.6 convolution_subtract_fusion.1
  40.8 0.2 broadcast_multiply_fusion
  41.1 1.0 fusion.33
  42.2 2.0 %fusion.42 = f32[2,8,128,128]{3,2,1,0:T(8,128)S(1)} fusion(f32[2,8,64,256]{3,2,1,0:T(8,128)S(1)} %fusion.33, f32[2,8,64]{2,1,0:T(8,128)S(1)} %get-tuple-element.25, f32[8,64,128]{2,1,0:T(8,128)S(1)} %convert_multiply_fusion.2), kind=kOutput, calls=%fused_computation.52 | convolution fusion | flops 201457664 | bytes 1843200 | tf_op jit(solution)/shard_map/hntd,hnte->hnde/dot_general | solution.py:127
  44.1 2.2 %convolution_subtract_fusion = f32[2,8,128,128]{3,2,1,0:T(8,128)S(1)} fusion(f32[128,128]{1,0:T(8,128)S(1)} %fusion.148, f32[2,8]{1,0:T(2,128)S(1)} %slice_reduce_fusion, f32[2,8,64,256]{3,2,1,0:T(8,128)S(1)} %fusion.33, f32[2,8,64]{2,1,0:T(8,128)S(1)} %get-tuple-element.25, f32[8,64,128]{2,1,0:T(8,128)S(1)} %convert_multiply_fusion.2), kind=kOutput, calls=%fused_computation.22 | convolution fusion | flops 201981952 | bytes 1909760 | tf_op jit(solution)/shard_map/hntd,hnte->hnde/dot_general | solution.py:124
  46.4 0.3 bitcast_dynamic-update-slice_fusion.5
  46.6 0.3 bitcast_dynamic-update-slice_fusion.4
  46.9 0.3 bitcast_dynamic-update-slice_fusion.3
  47.2 0.3 bitcast_dynamic-update-slice_fusion.2
  47.5 0.3 bitcast_dynamic-update-slice_fusion.1
  47.7 0.3 bitcast_dynamic-update-slice_fusion
  48.0 0.3 fusion.30
  48.3 1.1 convolution_subtract_fusion.6
  49.4 0.8 fusion.80
  50.2 0.7 fusion.77
  50.8 1.0 fusion.53
  51.9 1.1 copy_bitcast_fusion
  52.9 4.3 %all-to-all-start.2 = ((bf16[8,64,256]{2,1,0:T(8,128)(2,1)}), bf16[8,64,256]{2,1,0:T(8,128)(2,1)S(1)}, u32[]{:S(2)}, u32[]{:S(2)}) async-start(bf16[8,64,256]{2,1,0:T(8,128)(2,1)} %copy_bitcast_fusion), calls=%async_computation.2 | async-start | bytes 524288 | tf_op jit(solution)/shard_map/all_to_all | solution.py:165
  57.3 1.1 fusion.27
  58.4 5.4 %all-to-all-done.2 = bf16[8,64,256]{2,1,0:T(8,128)(2,1)S(1)} async-done(((bf16[8,64,256]{2,1,0:T(8,128)(2,1)}), bf16[8,64,256]{2,1,0:T(8,128)(2,1)S(1)}, u32[]{:S(2)}, u32[]{:S(2)}) %all-to-all-start.2) | async-done | bytes 262176 | tf_op jit(solution)/shard_map/all_to_all | solution.py:165
  63.7 5.1 %multiply_reduce_fusion = (f32[64]{0:T(128)S(1)}, f32[64,2048]{1,0:T(8,128)S(1)}) fusion(bf16[8,64,256]{2,1,0:T(8,128)(2,1)S(1)} %all-to-all-done.2, bf16[8,256,2048]{2,1,0:T(8,128)(2,1)} %bitcast.282, bf16[1,64,2048]{2,1,0:T(8,128)(2,1)S(1)} %copy-done.3), kind=kOutput, calls=%fused_computation.77 | convolution fusion | flops 537395136 | bytes 9437440 | tf_op jit(solution)/shard_map/jtf,jfd->td/dot_general | solution.py:166
  68.8 0.8 copy-done.1
  69.6 1.0 convolution_convert_fusion
  70.7 3.2 %copy.160 = bf16[128,3,2,2048]{3,2,1,0:T(2,128)(2,1)S(1)} copy(bf16[128,3,2,2048]{3,0,1,2:T(8,128)(2,1)S(1)} %convolution_convert_fusion) | data formatting | bytes 6291456 | tf_op jit(solution)/shard_map/convert_element_type | solution.py:190
  73.9 50.1 %all_to_all.25 = bf16[128,3,2,2048]{3,2,1,0:T(2,128)(2,1)S(1)} all-to-all(bf16[128,3,2,2048]{3,2,1,0:T(2,128)(2,1)S(1)} %copy.160), channel_id=1, replica_groups=mesh['ctx'=8,'req'=16] {'ctx','req'}, dimensions={0} | all-to-all | bytes 6291456 | tf_op jit(solution)/shard_map/all_to_all | solution.py:191
  124.1 4.1 %fusion = f32[2,128,3,1024]{3,1,2,0:T(8,128)S(1)} fusion(bf16[2,2048,1024]{2,1,0:T(8,128)(2,1)S(1)} %bitcast.304, bf16[128,3,2,2048]{3,2,1,0:T(2,128)(2,1)S(1)} %all_to_all.25), kind=kOutput, calls=%fused_computation | convolution fusion | flops 3221225472 | bytes 14680064 | tf_op jit(solution)/shard_map/scex,exf->escf/dot_general | solution.py:194
  128.2 1.9 %fusion.10 = bf16[128,3,2,2048]{3,0,2,1:T(8,128)(2,1)S(1)} fusion(bf16[2,512,2048]{2,1,0:T(8,128)(2,1)S(1)} %copy-done.8, f32[2,128,3,1024]{3,1,2,0:T(8,128)S(1)} %fusion), kind=kOutput, calls=%fused_computation.9 | convolution fusion | flops 1614544896 | bytes 10485760 | tf_op jit(solution)/shard_map/escf,efx->scex/dot_general | solution.py:198
  130.1 4.9 %copy.163 = bf16[128,3,2,2048]{3,2,1,0:T(2,128)(2,1)} copy(bf16[128,3,2,2048]{3,0,2,1:T(8,128)(2,1)S(1)} %fusion.10) | data formatting | bytes 6291456 | tf_op jit(solution)/shard_map/convert_element_type | solution.py:200
  135.0 4.9 %all-to-all-start.4 = ((bf16[128,3,2,2048]{3,2,1,0:T(2,128)(2,1)}), bf16[128,3,2,2048]{3,2,1,0:T(2,128)(2,1)S(1)}, u32[]{:S(2)}, u32[]{:S(2)}) async-start(bf16[128,3,2,2048]{3,2,1,0:T(2,128)(2,1)} %copy.163), calls=%async_computation.4 | async-start | bytes 6291456 | tf_op jit(solution)/shard_map/all_to_all | solution.py:201
  140.6 0.2 fusion.161
  140.9 1.6 dynamic-slice_bitcast_fusion
  142.4 1.0 copy.165
  143.4 2.0 %fusion.32 = f32[1,2,128,128]{2,3,1,0:T(8,128)} fusion(f32[2,128,128]{1,2,0:T(8,128)S(1)} %copy.165, f32[2,8,64,128]{3,2,1,0:T(8,128)} %copy-done.2, s32[]{:T(128)S(6)} %select_n.342, f32[2]{0:T(128)S(1)} %get-tuple-element.17, f32[8,64,128]{2,1,0:T(8,128)S(1)} %convert_multiply_fusion.2, f32[2,64]{1,0:T(2,128)S(1)} %multiply_select_fusion.6), kind=kOutput, calls=%fused_computation.40 | convolution fusion | flops 25247744 | bytes 363008 | tf_op jit(solution)/shard_map/td,hte->hde/dot_general | solution.py:156
  145.4 1.7 copy.166
  147.1 33.6 %all-to-all-done.4 = bf16[128,3,2,2048]{3,2,1,0:T(2,128)(2,1)S(1)} async-done(((bf16[128,3,2,2048]{3,2,1,0:T(2,128)(2,1)}), bf16[128,3,2,2048]{3,2,1,0:T(2,128)(2,1)S(1)}, u32[]{:S(2)}, u32[]{:S(2)}) %all-to-all-start.4) | async-done | bytes 3145760 | tf_op jit(solution)/shard_map/all_to_all | solution.py:201
  180.7 5.1 %fusion.23 = bf16[1,64,2048]{2,1,0:T(8,128)(2,1)} fusion(f32[64,2048]{1,0:T(8,128)} %copy-done.1, f32[128,3,2,64]{0,3,2,1:T(8,128)} %get-tuple-element.15, bf16[128,3,2,2048]{3,2,1,0:T(2,128)(2,1)S(1)} %all-to-all-done.4), kind=kOutput, calls=%fused_computation.17 | convolution fusion | flops 1208221696 | bytes 4128768 | tf_op jit(solution)/shard_map/dcet,dcex->tx/dot_general | solution.py:205
  (79 shorter events, 2.4 us)
Async XLA Ops:
  0.6 11.7 %copy-start.4 = (bf16[1,64,1024]{2,1,0:T(8,128)(2,1)S(1)}, bf16[1,64,1024]{2,1,0:T(8,128)(2,1)}, u32[]{:S(2)}) copy-start(bf16[1,64,1024]{2,1,0:T(8,128)(2,1)} %param.16) | copy-start | bytes 393220
  2.1 12.9 %all-to-all-start = ((f32[8,1,256]{2,1,0:T(1,128)}), f32[8,1,256]{2,1,0:T(1,128)S(1)}, u32[]{:S(2)}, u32[]{:S(2)}) async-start(f32[8,1,256]{2,1,0:T(1,128)} %reshape.881), calls=%async_computation | async-start | bytes 16384 | tf_op jit(solution)/shard_map/all_to_all | solution.py:93
  12.3 1.1 copy-start.5
  15.0 17.0 %all-to-all-start.1 = ((bf16[8,64,768]{2,1,0:T(8,128)(2,1)}), bf16[8,64,768]{2,1,0:T(8,128)(2,1)S(1)}, u32[]{:S(2)}, u32[]{:S(2)}) async-start(bf16[8,64,768]{2,1,0:T(8,128)(2,1)} %maximum_bitcast_fusion), calls=%async_computation.1 | async-start | bytes 1572864 | tf_op jit(solution)/shard_map/all_to_all | solution.py:89
  48.3 4.6 %copy-start = (f32[2,8,128,128]{3,2,0,1:T(8,128)}, f32[2,8,128,128]{3,2,0,1:T(8,128)S(1)}, u32[]{:S(2)}) copy-start(f32[2,8,128,128]{3,2,0,1:T(8,128)S(1)} %fusion.30) | copy-start | bytes 3145732
  48.3 3.6 %copy-start.7 = (f32[128]{0:T(128)S(1)}, f32[128]{0:T(128)}, u32[]{:S(2)}) copy-start(f32[128]{0:T(128)} %param.21) | copy-start | bytes 1540
  49.4 3.6 %copy-start.2 = (f32[2,8,64,128]{3,2,1,0:T(8,128)}, f32[2,8,64,128]{3,2,1,0:T(8,128)S(1)}, u32[]{:S(2)}) copy-start(f32[2,8,64,128]{3,2,1,0:T(8,128)S(1)} %convolution_subtract_fusion.6) | copy-start | bytes 1572868
  49.4 14.3 %copy-start.3 = (bf16[1,64,2048]{2,1,0:T(8,128)(2,1)S(1)}, bf16[1,64,2048]{2,1,0:T(8,128)(2,1)}, u32[]{:S(2)}) copy-start(bf16[1,64,2048]{2,1,0:T(8,128)(2,1)} %param.23) | copy-start | bytes 786436
  52.9 10.8 %all-to-all-start.2 = ((bf16[8,64,256]{2,1,0:T(8,128)(2,1)}), bf16[8,64,256]{2,1,0:T(8,128)(2,1)S(1)}, u32[]{:S(2)}, u32[]{:S(2)}) async-start(bf16[8,64,256]{2,1,0:T(8,128)(2,1)} %copy_bitcast_fusion), calls=%async_computation.2 | async-start | bytes 524288 | tf_op jit(solution)/shard_map/all_to_all | solution.py:165
  63.7 5.9 %copy-start.6 = (f32[2048]{0:T(1024)S(1)}, f32[2048]{0:T(1024)}, u32[]{:S(2)}) copy-start(f32[2048]{0:T(1024)} %param.24) | copy-start | bytes 24580
  68.8 0.8 copy-start.1
  69.6 54.4 %slice-start = ((s8[8388608]{0:T(1024)(128)(4,1)}), s8[4194304]{0:T(1024)(128)(4,1)S(1)}, s32[]{:S(2)}) async-start(s8[8388608]{0:T(1024)(128)(4,1)} %bitcast.303), calls=%async_computation.5 | async-start | bytes 8388608
  70.7 53.4 %slice-start.1 = ((s8[8388608]{0:T(1024)(128)(4,1)}), s8[4194304]{0:T(1024)(128)(4,1)S(1)}, s32[]{:S(2)}) async-start(s8[8388608]{0:T(1024)(128)(4,1)} %bitcast.303), calls=%async_computation.6 | async-start | bytes 8388608
  124.1 4.1 %copy-start.8 = (bf16[2,512,2048]{2,1,0:T(8,128)(2,1)S(1)}, bf16[2,512,2048]{2,1,0:T(8,128)(2,1)}, u32[]{:S(2)}) copy-start(bf16[2,512,2048]{2,1,0:T(8,128)(2,1)} %param.28) | copy-start | bytes 12582916
  135.0 45.7 %all-to-all-start.4 = ((bf16[128,3,2,2048]{3,2,1,0:T(2,128)(2,1)}), bf16[128,3,2,2048]{3,2,1,0:T(2,128)(2,1)S(1)}, u32[]{:S(2)}, u32[]{:S(2)}) async-start(bf16[128,3,2,2048]{3,2,1,0:T(2,128)(2,1)} %copy.163), calls=%async_computation.4 | async-start | bytes 6291456 | tf_op jit(solution)/shard_map/all_to_all | solution.py:201
